TPU v7x, 128 devices: a whole 4x4x4 slice. The times are simulated.
128 devices in a mesh: req: 4 (over y), exp: 32 (over z, x, core).
Axes of the slice: x: 4, y: 4, z: 4, core: 2. Of those that a mesh axis runs over, the one named last changes fastest.
Arguments:
- states: bfloat16 [2, 16384, 1024], P(None, ('req', 'exp')), may hold values from -6 to 6
- lengths: int32 [128, 4], P(('req', 'exp')), may hold values from 1 to 64, 128 in all within a row
- targets: int32 [16384], P('req'), may hold values from 0 to 36863
- routes: int32 [2, 16384, 8], P(None, ('req', 'exp')), may hold values from 0 to 31, all different within a row; in each aligned block of 128 rows (0 to 127, 128 to 255, ..., all dimensions but the last counted through in order) at most 40 rows name the same one
- gate_probs: float32 [2, 16384, 8], P(None, ('req', 'exp')), may hold values from 0.02 to 0.4
- owners: int32 [512], P(('req', 'exp')), may hold values from 0 to 511, each once
- norm_gains: float32 [2, 3, 1024], replicated, may hold values from 0.25 to 1.75
- qkv_weight: bfloat16 [2, 1024, 2048], replicated, may hold values from -14 to 14
- out_weight: bfloat16 [2, 1024, 1024], replicated, may hold values from -0.1875 to 0.1875
- expert_in: bfloat16 [2, 32, 1024, 1024], P(None, 'exp'), may hold values from -0.1875 to 0.1875
- expert_down: bfloat16 [2, 32, 512, 1024], P(None, 'exp'), may hold values from -0.25 to 0.25
- vocab_head: bfloat16 [2, 36864, 1024], P(None, 'exp'), may hold values from -170 to 170
Outputs:
- token_logp: float32 [2, 16384], P(None, ('req', 'exp'))
- seq_totals: float32 [512], P(('req', 'exp'))
Inputs may be any that keep to these rules, and one draw needn't show every extreme that they name: `lengths`: each row sums to 128; some row reaches 64. `routes`: the 8 experts of a token are distinct; among the 128 tokens of one device, no expert is named by more than 40 of them for one model, and that bound is reached. `owners`: a permutation of the sequence numbers.
All inputs are finite; a program needn't handle non-finite values.
Results may differ from a plain program's by a relative error of at most 0.012.
The roundings to bfloat16 on the way count: a program that leaves them out, or rounds other values in their place, can miss the bound.
Values may be sent and summed in bfloat16 or wider, within the bound.
No kernel may reach another device: no remote copies, remote signals or barrier semaphores. Data moves between devices by JAX's collectives and lax.ppermute only.
A program may use at most 128 MiB of HBM per device.

v0:
```python
import jax
import jax.numpy as jnp
from jax import lax
from jax.sharding import PartitionSpec as P

HEADS = 16
KV_HEADS = 8
HEAD_DIM = 64
EXPERT_FF = 512
EXPERTS = 32
TOP = 8
CAP = 40
EPSILON = 1e-06
RESIDUAL_SCALE = 0.22
SCORE_SCALE = 0.015625
LOGIT_DIVISOR = 6.0
ROTARY_BASE = 10000.0


def combined_all(x, axis, combine):
    everything = jax.tree.map(lambda part: lax.all_gather(part, axis), x)
    initial = jax.tree.map(lambda part: part[0], everything)

    def step(k, so_far):
        return combine(so_far, jax.tree.map(lambda part: part[k], everything))

    return lax.fori_loop(1, lax.axis_size(axis), step, initial)


def root_norm(values, gain_row):
    values = values.astype(jnp.float32)
    scaled = lax.rsqrt(jnp.mean(values * values, axis=-1, keepdims=True) + EPSILON)
    return values * scaled * gain_row


def segment_table(length_row, token_count):
    seq_ends = jnp.cumsum(length_row)
    seq_starts = seq_ends - length_row
    places = jnp.arange(token_count, dtype=jnp.int32)
    segment = jnp.sum((places[:, None] >= seq_ends[None, :]).astype(jnp.int32), axis=1)
    member = segment[:, None] == jnp.arange(length_row.shape[0], dtype=jnp.int32)[None, :]
    position = places - jnp.sum(member.astype(jnp.int32) * seq_starts[None, :], axis=1)
    return (segment, member, position)


def rotary(values, position):
    half_dim = values.shape[-1] // 2
    frequency = ROTARY_BASE ** (-2.0 * jnp.arange(half_dim, dtype=jnp.float32) / values.shape[-1])
    angles = position.astype(jnp.float32)[:, None] * frequency[None, :]
    angles = jnp.concatenate([angles, angles], axis=-1)[:, None, :]
    leading = values[..., :half_dim]
    trailing = values[..., half_dim:]
    turned = jnp.concatenate([-trailing, leading], axis=-1)
    return values * jnp.cos(angles) + turned * jnp.sin(angles)


def attend(block_states, segment, position, gain_row, qkv_weight, out_weight):
    token_count = block_states.shape[0]
    group_size = HEADS // KV_HEADS
    normed = root_norm(block_states, gain_row).astype(jnp.bfloat16)
    mixed = jnp.dot(normed, qkv_weight, preferred_element_type=jnp.float32)
    queries = rotary(
        mixed[:, : HEADS * HEAD_DIM].reshape(token_count, HEADS, HEAD_DIM), position
    ).astype(jnp.bfloat16)
    keys_all = rotary(
        mixed[:, HEADS * HEAD_DIM : (HEADS + KV_HEADS) * HEAD_DIM].reshape(
            token_count, KV_HEADS, HEAD_DIM
        ),
        position,
    ).astype(jnp.bfloat16)
    values_all = (
        mixed[:, (HEADS + KV_HEADS) * HEAD_DIM :]
        .reshape(token_count, KV_HEADS, HEAD_DIM)
        .astype(jnp.bfloat16)
    )
    grouped = queries.reshape(token_count, KV_HEADS, group_size, HEAD_DIM)
    scores = (
        jnp.einsum("tgqd,sgd->gqts", grouped, keys_all, preferred_element_type=jnp.float32)
        * SCORE_SCALE
    )
    places = jnp.arange(token_count, dtype=jnp.int32)
    allowed = (segment[:, None] == segment[None, :]) & (places[None, :] <= places[:, None])
    scores = jnp.where(allowed, scores, -1e30)
    highest = jnp.max(scores, axis=-1, keepdims=True)
    weights = jnp.exp(scores - highest)
    weights = (weights / jnp.sum(weights, axis=-1, keepdims=True)).astype(jnp.bfloat16)
    attended = jnp.einsum(
        "gqts,sgd->tgqd", weights, values_all, preferred_element_type=jnp.float32
    ).astype(jnp.bfloat16)
    projected = jnp.dot(
        attended.reshape(token_count, HEADS * HEAD_DIM),
        out_weight,
        preferred_element_type=jnp.float32,
    )
    return (block_states.astype(jnp.float32) + RESIDUAL_SCALE * projected).astype(jnp.bfloat16)


def join_parts(first_part, second_part):
    first_max, first_mass, first_hit = first_part
    second_max, second_mass, second_hit = second_part
    joined_max = jnp.maximum(first_max, second_max)
    joined_mass = first_mass * jnp.exp(first_max - joined_max) + second_mass * jnp.exp(
        second_max - joined_max
    )
    return (joined_max, joined_mass, first_hit + second_hit)


def per_device(
    states,
    lengths,
    targets,
    routes,
    gate_probs,
    owners,
    norm_gains,
    qkv_weight,
    out_weight,
    expert_in,
    expert_down,
    vocab_head,
):
    token_count = states.shape[1]
    width = states.shape[2]
    segment, member, position = segment_table(lengths[0], token_count)
    residual = jnp.stack(
        [
            attend(
                states[which],
                segment,
                position,
                norm_gains[which, 0],
                qkv_weight[which],
                out_weight[which],
            )
            for which in range(2)
        ]
    )
    moe_in = root_norm(residual, norm_gains[:, 1][:, None, :]).astype(jnp.bfloat16)
    groups = lax.axis_size("exp")
    local_count = expert_in.shape[1]
    flat_routes = routes.reshape(2, token_count * TOP)
    onehot = (flat_routes[..., None] == jnp.arange(EXPERTS, dtype=jnp.int32)).astype(jnp.int32)
    rank_slot = jnp.sum((jnp.cumsum(onehot, axis=1) - 1) * onehot, axis=2)
    slot_index = (
        flat_routes * CAP + rank_slot + jnp.arange(2, dtype=jnp.int32)[:, None] * (EXPERTS * CAP)
    ).reshape(-1)
    token_index = jnp.arange(token_count * TOP, dtype=jnp.int32) // TOP
    outgoing = (
        jnp.zeros((2 * EXPERTS * CAP, width), jnp.bfloat16)
        .at[slot_index]
        .set(moe_in[:, token_index].reshape(-1, width))
    )
    arrived = lax.all_to_all(
        outgoing.reshape(2, groups, local_count * CAP, width),
        "exp",
        split_axis=1,
        concat_axis=1,
        tiled=True,
    )
    inputs = arrived.reshape(2, groups, local_count, CAP, width)
    gate_up = jnp.einsum("mslcd,mldf->mslcf", inputs, expert_in, preferred_element_type=jnp.float32)
    hidden = (jax.nn.silu(gate_up[..., :EXPERT_FF]) * gate_up[..., EXPERT_FF:]).astype(jnp.bfloat16)
    produced = jnp.einsum(
        "mslcf,mlfd->mslcd", hidden, expert_down, preferred_element_type=jnp.float32
    ).astype(jnp.bfloat16)
    returned = lax.all_to_all(
        produced.reshape(2, groups, local_count * CAP, width),
        "exp",
        split_axis=1,
        concat_axis=1,
        tiled=True,
    )
    picked = returned.reshape(2 * EXPERTS * CAP, width)[slot_index].reshape(
        2, token_count, TOP, width
    )
    mixture = jnp.sum(gate_probs[..., None] * picked.astype(jnp.float32), axis=2)
    final = root_norm(
        residual.astype(jnp.float32) + RESIDUAL_SCALE * mixture, norm_gains[:, 2][:, None, :]
    ).astype(jnp.bfloat16)
    shard = lax.axis_index("exp")
    vocab_rows = vocab_head.shape[1]
    lowest = shard * vocab_rows
    vocab_ids = jnp.arange(vocab_rows, dtype=jnp.int32)
    shard_piece = lax.all_gather(final, "exp", axis=1, tiled=True)
    piece_rows = shard_piece.shape[1]
    block_rows = 512
    block_count = piece_rows // block_rows
    wanted_all = targets - lowest

    def one_block(block_number):
        row_block = lax.dynamic_slice_in_dim(shard_piece, block_number * block_rows, block_rows, 1)
        wanted = lax.dynamic_slice_in_dim(wanted_all, block_number * block_rows, block_rows, 0)
        logits = (
            jnp.einsum("mtd,mvd->mtv", row_block, vocab_head, preferred_element_type=jnp.float32)
            / LOGIT_DIVISOR
        )
        highest = jnp.max(logits, axis=2)
        masses = jnp.sum(jnp.exp(logits - highest[..., None]), axis=2)
        chosen = jnp.sum(
            jnp.where(wanted[None, :, None] == vocab_ids[None, None, :], logits, 0.0), axis=2
        )
        return (highest, masses, chosen)

    block_max, block_mass, block_hit = lax.map(one_block, jnp.arange(block_count, dtype=jnp.int32))

    def place(fresh):
        ordered = jnp.transpose(fresh, (1, 0, 2)).reshape(2, piece_rows)
        return ordered

    part_max = place(block_max)
    part_mass = place(block_mass)
    part_hit = place(block_hit)
    all_max, all_mass, all_hit = combined_all((part_max, part_mass, part_hit), "exp", join_parts)
    begin = shard * token_count
    final_max = lax.dynamic_slice_in_dim(all_max, begin, token_count, 1)
    final_mass = lax.dynamic_slice_in_dim(all_mass, begin, token_count, 1)
    final_hit = lax.dynamic_slice_in_dim(all_hit, begin, token_count, 1)
    token_logp = final_hit - (final_max + jnp.log(final_mass))
    difference = token_logp[0] - token_logp[1]
    seq_sums = jnp.sum(member.astype(jnp.float32) * difference[:, None], axis=0)
    devices = lax.axis_size("req") * lax.axis_size("exp")
    everyone = devices * seq_sums.shape[0]
    dense_totals = jnp.sum(
        (owners[:, None] == jnp.arange(everyone, dtype=jnp.int32)[None, :]).astype(jnp.float32)
        * seq_sums[:, None],
        axis=0,
    )
    seq_totals = lax.psum_scatter(dense_totals, ("req", "exp"), scatter_dimension=0, tiled=True)
    return (token_logp, seq_totals)


def solution(mesh):
    in_specs = (
        P(None, ("req", "exp"), None),
        P(("req", "exp"), None),
        P("req"),
        P(None, ("req", "exp"), None),
        P(None, ("req", "exp"), None),
        P(("req", "exp")),
        P(),
        P(),
        P(),
        P(None, "exp", None, None),
        P(None, "exp", None, None),
        P(None, "exp", None),
    )
    out_specs = (P(None, ("req", "exp")), P(("req", "exp")))
    return jax.shard_map(
        per_device, mesh=mesh, in_specs=in_specs, out_specs=out_specs, check_vma=False
    )
```

profile of v0, /device:TPU:1, one launch (start us, length us, event | category | flops | bytes accessed | tf_op | source)
XLA Modules:
  0.0 671.6 jit_solution(7500306601122006520)
XLA Ops:
  9.4 3.1 fusion.15
  15.6 2.3 fusion.42
  17.9 2.1 fusion.144
  20.0 1.6 slice.227
  21.6 3.1 fusion.13
  26.8 2.4 fusion.40
  29.2 2.1 fusion.139
  36.7 2.7 convolution_convert_fusion.2
  39.4 2.2 fusion.61
  41.6 2.8 convolution_convert_fusion.1
  44.4 2.2 fusion.64
  47.5 15.8 %gather_fusion = bf16[1024,2,1024]{2,1,0:T(2,128)(2,1)} fusion(bf16[2,128,1024]{2,0,1:T(2,128)(2,1)S(1)} %copy.125, s32[1024]{0:T(1024)S(1)} %broadcast_clamp_fusion.1), kind=kCustom, calls=%fused_computation | custom fusion | bytes 8392704 | tf_op jit(solution)/shard_map/gather | solution.py:151
  63.3 5.6 copy.126
  68.9 18.0 %reduce-window.11 = s32[2,32,8,128]{3,2,1,0:T(8,128)S(1)} reduce-window(s32[2,32,8,128]{3,2,1,0:T(8,128)S(1)} %fusion.101, s32[]{:T(128)} %constant.119.clone.1), window={size=1x1x1x128 pad=0_0x0_0x0_0x127_0}, to_apply=%region_9.10 | reduce-window | flops 8323072 | bytes 524292 | tf_op jit(solution)/shard_map/reduce-window.1
  88.0 13.6 %scatter_custom_fusion = bf16[2560,1024]{1,0:T(8,128)(2,1)} fusion(s32[2048]{0:T(1024)S(1)} %bitcast.262, bf16[2048,1024]{1,0:T(8,128)(2,1)} %bitcast.240, bf16[]{:T(256)} %constant.129.clone.1), kind=kCustom, calls=%fused_computation.37 | custom fusion | bytes 5243392 | tf_op jit(solution)/shard_map/scatter | solution.py:151
  101.7 3.3 copy.127
  105.0 71.5 %all_to_all.10 = bf16[2,32,40,1024]{3,2,0,1:T(8,128)(2,1)S(1)} all-to-all(bf16[2,32,40,1024]{3,2,0,1:T(8,128)(2,1)S(1)} %copy.127), channel_id=1, replica_groups=mesh['req'=4,'exp'=32] {'exp'}, dimensions={1} | all-to-all | bytes 10485760 | tf_op jit(solution)/shard_map/all_to_all | solution.py:153
  176.5 8.2 %fusion.19 = f32[2,32,1,40,1024]{4,3,1,0,2:T(8,128)} fusion(bf16[2,1,1024,1024]{3,2,1,0:T(8,128)(2,1)S(1)} %copy-done.20, bf16[2,32,40,1024]{3,2,0,1:T(8,128)(2,1)S(1)} %all_to_all.10), kind=kOutput, calls=%fused_computation.34 | convolution fusion | flops 5368709120 | bytes 19922944 | tf_op jit(solution)/shard_map/mslcd,mldf->mslcf/dot_general | solution.py:161
  184.7 7.2 %convolution_convert_fusion = bf16[2,32,40,1024]{3,2,1,0:T(8,128)(2,1)S(1)} fusion(f32[2,32,1,40,1024]{4,3,1,0,2:T(8,128)} %fusion.19, bf16[2,1,512,1024]{3,2,1,0:T(8,128)(2,1)S(1)} %copy-done), kind=kOutput, calls=%fused_computation.35 | convolution fusion | flops 2694840320 | bytes 17825792 | tf_op jit(solution)/shard_map/mslcf,mlfd->mslcd/dot_general | solution.py:163
  191.8 3.2 copy.129
  195.0 5.0 all-to-all-start.1
  200.2 61.7 %all-to-all-done.1 = bf16[2,32,40,1024]{3,2,0,1:T(8,128)(2,1)} async-done(((bf16[2,32,40,1024]{3,2,0,1:T(8,128)(2,1)}), bf16[2,32,40,1024]{3,2,0,1:T(8,128)(2,1)}, u32[]{:S(2)}, u32[]{:S(2)}) %all-to-all-start.1) | async-done | bytes 5242912 | tf_op jit(solution)/shard_map/all_to_all | solution.py:166
  261.9 5.6 copy.130
  267.5 14.1 %gather_fusion.1 = bf16[2048,1024]{1,0:T(8,128)(2,1)} fusion(bf16[2560,1024]{1,0:T(8,128)(2,1)} %bitcast.231, s32[2048]{0:T(1024)S(1)} %broadcast_clamp_fusion), kind=kCustom, calls=%fused_computation.1 | custom fusion | bytes 8396800 | tf_op jit(solution)/shard_map/gather | solution.py:173
  281.6 4.8 fusion.8
  287.8 73.6 %all-gather.5.cloned.1.call-done = bf16[2,4096,1024]{2,1,0:T(8,128)(2,1)} async-done(((bf16[2,128,1024]{2,1,0:T(8,128)(2,1)}), bf16[2,4096,1024]{2,1,0:T(8,128)(2,1)}) %all-gather.5.cloned.1.call-update) | async-done | bytes 16777232 | tf_op jit(solution)/shard_map/all_gather | solution.py:184
  361.4 79.6 %while.35 = (s32[]{:T(128)}, f32[8,2,512]{2,1,0:T(2,128)S(1)}, f32[8,2,512]{2,1,0:T(2,128)}, f32[8,2,512]{2,1,0:T(2,128)}, s32[8]{0:T(128)S(1)}, /*index=5*/bf16...) while((s32[]{:T(128)}, f32[8,2,512]{2,1,0:T(2,128)S(1)}, ...), condition=%wide.region_20.21_spmd.clone, body=%wide.region_16.20_spmd.clone.sunk | while | flops 2423583744 | bytes 17480380 | solution.py:204
  362.7 6.0 fusion.161
  369.1 1.6 select_reduce_fusion.5
  372.6 6.0 fusion.161
  379.1 1.6 select_reduce_fusion.5
  382.6 6.0 fusion.161
  389.0 1.6 select_reduce_fusion.5
  392.5 6.0 fusion.161
  399.0 1.6 select_reduce_fusion.5
  402.5 6.0 fusion.161
  408.9 1.6 select_reduce_fusion.5
  412.4 6.0 fusion.161
  418.9 1.6 select_reduce_fusion.5
  422.4 6.0 fusion.161
  428.8 1.6 select_reduce_fusion.5
  432.3 6.0 fusion.161
  438.8 1.6 select_reduce_fusion.5
  442.4 40.9 %all-gather.11.cloned.1.call-done = f32[32,2,4096]{2,1,0:T(2,128)} async-done(((f32[1,2,4096]{2,1,0:T(2,128)}), f32[32,2,4096]{2,1,0:T(2,128)}) %all-gather.11.cloned.1.call-update) | async-done | bytes 1048592 | tf_op jit(solution)/shard_map/all_gather | solution.py:21
  484.0 43.5 %all-gather.9.cloned.1.call-done = f32[32,2,4096]{2,1,0:T(2,128)} async-done(((f32[1,2,4096]{2,1,0:T(2,128)}), f32[32,2,4096]{2,1,0:T(2,128)}) %all-gather.9.cloned.1.call-update) | async-done | bytes 1048592 | tf_op jit(solution)/shard_map/all_gather | solution.py:21
  528.2 43.4 %all-gather.7.cloned.1.call-done = f32[32,2,4096]{2,1,0:T(2,128)} async-done(((f32[1,2,4096]{2,1,0:T(2,128)}), f32[32,2,4096]{2,1,0:T(2,128)}) %all-gather.7.cloned.1.call-update) | async-done | bytes 1048592 | tf_op jit(solution)/shard_map/all_gather | solution.py:21
  572.4 27.7 %while.34 = (s32[]{:T(128)}, f32[2,4096]{1,0:T(2,128)S(1)}, f32[2,4096]{1,0:T(2,128)S(1)}, f32[2,4096]{1,0:T(2,128)S(1)}, f32[32,2,4096]{2,1,0:T(2,128)}, /*inde...) while((s32[]{:T(128)}, f32[2,4096]{1,0:T(2,128)S(1)}, ...), condition=%wide.region_22.23_spmd, body=%wide.region_21.22_spmd.sunk | while | flops 57349 | bytes 295059 | solution.py:27
  600.3 64.1 %all-reduce = f32[512]{0:T(512)S(1)} all-reduce(f32[512]{0:T(512)S(1)} %select_reduce_fusion.1), channel_id=2, replica_groups=mesh['req'=4,'exp'=32] {'req','exp'}, use_global_device_ids=true, to_apply=%region_25.26.clone | all-reduce | flops 512 | bytes 4096
  (195 shorter events, 61.3 us)
Async XLA Ops:
  7.2 177.5 %copy-start = (bf16[2,1,512,1024]{3,2,1,0:T(8,128)(2,1)S(1)}, bf16[2,1,512,1024]{3,2,1,0:T(8,128)(2,1)}, u32[]{:S(2)}) copy-start(bf16[2,1,512,1024]{3,2,1,0:T(8,128)(2,1)} %param.26) | copy-start | bytes 6291460
  9.3 5.2 copy-start.21
  12.4 1.0 copy-start.2
  14.9 0.6 copy-start.15
  24.7 1.0 copy-start.3
  25.7 6.6 copy-start.11
  25.7 7.2 %copy-start.8 = (s32[2,128,8]{1,2,0:T(8,128)S(1)}, s32[2,128,8]{1,2,0:T(8,128)}, u32[]{:S(2)}) copy-start(s32[2,128,8]{1,2,0:T(8,128)} %param.19) | copy-start | bytes 24580
  31.3 8.2 %copy-start.4 = (bf16[2,128,1024]{2,1,0:T(8,128)(2,1)S(1)}, bf16[2,128,1024]{2,1,0:T(8,128)(2,1)}, u32[]{:S(2)}) copy-start(bf16[2,128,1024]{2,1,0:T(8,128)(2,1)} %param.16) | copy-start | bytes 1572868
  39.4 5.0 copy-start.5
  41.6 5.9 copy-start.13
  63.3 5.6 copy-start.7
  63.3 24.2 %copy-start.6 = (s32[2,1024]{1,0:T(2,128)S(1)}, s32[2,1024]{1,0:T(2,128)}, u32[]{:S(2)}) copy-start(s32[2,1024]{1,0:T(2,128)} %eq.95) | copy-start | bytes 24580
  63.3 24.3 %copy-start.9 = (s32[2,128,8]{1,2,0:T(8,128)S(1)}, s32[2,128,8]{1,2,0:T(8,128)}, u32[]{:S(2)}) copy-start(s32[2,128,8]{1,2,0:T(8,128)} %broadcast_multiply_fusion.1) | copy-start | bytes 24580
  63.3 24.6 %copy-start.18 = (s32[2]{0:T(128)S(1)}, s32[2]{0:T(128)}, u32[]{:S(2)}) copy-start(s32[2]{0:T(128)} %iota_multiply_fusion) | copy-start | bytes 28
  105.0 71.5 %copy-start.20 = (bf16[2,1,1024,1024]{3,2,1,0:T(8,128)(2,1)S(1)}, bf16[2,1,1024,1024]{3,2,1,0:T(8,128)(2,1)}, u32[]{:S(2)}) copy-start(bf16[2,1,1024,1024]{3,2,1,0:T(8,128)(2,1)} %param.25) | copy-start | bytes 12582916
  195.0 5.0 copy-start.14
  195.0 66.9 %all-to-all-start.1 = ((bf16[2,32,40,1024]{3,2,0,1:T(8,128)(2,1)}), bf16[2,32,40,1024]{3,2,0,1:T(8,128)(2,1)}, u32[]{:S(2)}, u32[]{:S(2)}) async-start(bf16[2,32,40,1024]{3,2,0,1:T(8,128)(2,1)} %copy.129), calls=%async_computation.1 | async-start | bytes 10485760 | tf_op jit(solution)/shard_map/all_to_all | solution.py:166
  200.0 161.4 %all-gather.5.cloned.1.call-start = ((), (), s32[]{:S(2)}) async-start(), calls=%async_computation.2 | async-start | bytes 17301504 | tf_op jit(solution)/shard_map/all_gather | solution.py:184
  281.6 6.2 copy-start.12
  287.7 195.5 %all-gather.11.cloned.1.call-start = ((), (), s32[]{:S(2)}) async-start(), calls=%async_computation.5 | async-start | bytes 1081344 | tf_op jit(solution)/shard_map/all_gather | solution.py:21
  361.4 238.7 %copy-start.16 = (s32[128]{0:T(128)S(1)}, s32[128]{0:T(128)}, u32[]{:S(2)}) copy-start(s32[128]{0:T(128)} %copy-done.15) | copy-start | bytes 1540
  361.4 238.8 %copy-start.19 = (s32[4]{0:T(128)S(1)}, s32[4]{0:T(128)}, u32[]{:S(2)}) copy-start(s32[4]{0:T(128)} %param.21) | copy-start | bytes 52
  441.0 0.8 copy-start.10
  441.0 224.0 %copy-start.1 = (bf16[2,1,512,1024]{3,2,1,0:T(8,128)(2,1)S(1)}, bf16[2,1,512,1024]{3,2,1,0:T(8,128)(2,1)}, u32[]{:S(2)}) copy-start(bf16[2,1,512,1024]{3,2,1,0:T(8,128)(2,1)} %param.26) | copy-start | bytes 6291460
  441.0 86.4 %all-gather.9.cloned.1.call-start = ((), (), s32[]{:S(2)}) async-start(), calls=%async_computation.4 | async-start | bytes 1081344 | tf_op jit(solution)/shard_map/all_gather | solution.py:21
  441.8 129.8 %all-gather.7.cloned.1.call-start = ((), (), s32[]{:S(2)}) async-start(), calls=%async_computation.3 | async-start | bytes 1081344 | tf_op jit(solution)/shard_map/all_gather | solution.py:21
  600.1 65.0 %copy-start.17 = (f32[2,128]{1,0:T(2,128)}, f32[2,128]{1,0:T(2,128)S(1)}, u32[]{:S(2)}) copy-start(f32[2,128]{1,0:T(2,128)S(1)} %add_subtract_fusion) | copy-start | bytes 3076
Sparse Core Ops, SparseCore 0:
  287.8 73.5 all-gather.4
  441.2 42.0 all-gather.10
  485.5 41.9 all-gather.8
  529.6 41.9 all-gather.6
where the time goes:
time: 675 us; the launch traced here: 672 us
  waiting for transfers between devices  264 us (39%)
  blocking collectives  136 us (20%)
  matrix products  88 us (13%)
  local copies, waits for them, and re-layouts  84.9 us (13%)
  other arithmetic  73.5 us (11%)
  between operations  14.3 us (2%)
    all_gather x3, waiting for transfers between devices, combined_all(): everything = jax.tree.map(lambda part: lax.all_gather(part, axis), x)  128 us
    all_gather x1, waiting for transfers between devices, per_device(): shard_piece = lax.all_gather(final, 'exp', axis=1, tiled=True)  73.6 us
    all_to_all x1, blocking collectives, per_device(): lax.all_to_all(outgoing.reshape(2, groups, local_count * CAP, width), 'ex...  71.5 us
    unnamed x1, blocking collectives  64.1 us
    all_to_all x1, waiting for transfers between devices, per_device(): lax.all_to_all(produced.reshape(2, groups, local_count * CAP, width), 'ex...  61.7 us
    dot_general x8, matrix products, one_block(): jnp.einsum('mtd,mvd->mtv', row_block, vocab_head, preferred_element_type=...  47.9 us
    add x31, other arithmetic, join_parts(): first_mass * jnp.exp(first_max - joined_max)  27.2 us
    gather x2, local copies, waits for them, and re-layouts, per_device(): moe_in[:, token_index].reshape(-1, width)  21.3 us
  transfers between devices with their start and end apart: 5, of which 5 were waited for; matrix products, arithmetic and copies ran while one was open for 0% of the time, Pallas kernels for 0%

commit v1 on v0

--- a/solution.py
+++ b/solution.py
@@ -163,12 +163,20 @@
     produced = jnp.einsum(
         "mslcf,mlfd->mslcd", hidden, expert_down, preferred_element_type=jnp.float32
     ).astype(jnp.bfloat16)
-    returned = lax.all_to_all(
-        produced.reshape(2, groups, local_count * CAP, width),
-        "exp",
-        split_axis=1,
-        concat_axis=1,
-        tiled=True,
+    returned = jnp.concatenate(
+        lax.all_to_all(
+            jnp.stack(
+                jnp.split(
+                    produced.reshape(2, groups, local_count * CAP, width),
+                    lax.axis_size("exp"),
+                    axis=1,
+                )
+            ),
+            "exp",
+            0,
+            0,
+        ),
+        axis=1,
     )
     picked = returned.reshape(2 * EXPERTS * CAP, width)[slot_index].reshape(
         2, token_count, TOP, width

time: 675 us -> 693 us (1.027)
  local copies, waits for them, and re-layouts: 84.9 us -> 103 us
    unnamed x50 -> x81, local copies, waits for them, and re-layouts: 3.31 us -> 24.3 us
where the time goes in v1:
time: 693 us; the launch traced here: 690 us
  waiting for transfers between devices  264 us (38%)
  blocking collectives  136 us (20%)
  local copies, waits for them, and re-layouts  103 us (15%)
  matrix products  88 us (13%)
  other arithmetic  73.5 us (11%)
  between operations  14.3 us (2%)
    all_gather x3, waiting for transfers between devices, combined_all(): everything = jax.tree.map(lambda part: lax.all_gather(part, axis), x)  128 us
    all_gather x1, waiting for transfers between devices, per_device(): shard_piece = lax.all_gather(final, 'exp', axis=1, tiled=True)  73.6 us
    all_to_all x1, blocking collectives, per_device(): lax.all_to_all(outgoing.reshape(2, groups, local_count * CAP, width), 'ex...  71.5 us
    unnamed x1, blocking collectives  64.1 us
    all_to_all x1, waiting for transfers between devices, per_device(): lax.all_to_all(jnp.stack(jnp.split(produced.reshape(2, groups, local_coun...  61.7 us
    dot_general x8, matrix products, one_block(): jnp.einsum('mtd,mvd->mtv', row_block, vocab_head, preferred_element_type=...  47.9 us
    add x31, other arithmetic, join_parts(): first_mass * jnp.exp(first_max - joined_max)  27.2 us
    unnamed x81, local copies, waits for them, and re-layouts  24.3 us
  transfers between devices with their start and end apart: 5, of which 5 were waited for; matrix products, arithmetic and copies ran while one was open for 0% of the time, Pallas kernels for 0%

profile of v1, /device:TPU:1, one launch (start us, length us, event | category | flops | bytes accessed | tf_op | source)
XLA Modules:
  0.0 690.0 jit_solution(15164467747743449619)
XLA Ops:
  7.2 1.4 fusion.72
  9.4 3.1 fusion.15
  15.6 2.3 fusion.42
  17.9 2.1 fusion.176
  20.0 1.6 slice.227
  21.6 3.1 fusion.13
  26.8 2.4 fusion.40
  29.2 2.1 fusion.171
  36.7 2.7 convolution_convert_fusion.2
  39.5 2.2 fusion.61
  41.6 2.8 convolution_convert_fusion.1
  44.4 2.2 fusion.64
  47.5 15.8 %gather_fusion = bf16[1024,2,1024]{2,1,0:T(2,128)(2,1)} fusion(bf16[2,128,1024]{2,0,1:T(2,128)(2,1)S(1)} %copy.280, s32[1024]{0:T(1024)S(1)} %broadcast_clamp_fusion.1), kind=kCustom, calls=%fused_computation | custom fusion | bytes 8392704 | tf_op jit(solution)/shard_map/gather | solution.py:151
  63.3 5.6 copy.281
  68.9 18.0 %reduce-window.11 = s32[2,32,8,128]{3,2,1,0:T(8,128)S(1)} reduce-window(s32[2,32,8,128]{3,2,1,0:T(8,128)S(1)} %fusion.101, s32[]{:T(128)} %constant.119.clone.1), window={size=1x1x1x128 pad=0_0x0_0x0_0x127_0}, to_apply=%region_9.10 | reduce-window | flops 8323072 | bytes 524292 | tf_op jit(solution)/shard_map/reduce-window.1
  88.0 13.6 %scatter_custom_fusion = bf16[2560,1024]{1,0:T(8,128)(2,1)} fusion(s32[2048]{0:T(1024)S(1)} %bitcast.453, bf16[2048,1024]{1,0:T(8,128)(2,1)} %bitcast.431, bf16[]{:T(256)} %constant.129.clone.1), kind=kCustom, calls=%fused_computation.37 | custom fusion | bytes 5243392 | tf_op jit(solution)/shard_map/scatter | solution.py:151
  101.7 3.3 copy.282
  105.0 71.5 %all_to_all.10 = bf16[2,32,40,1024]{3,2,0,1:T(8,128)(2,1)S(1)} all-to-all(bf16[2,32,40,1024]{3,2,0,1:T(8,128)(2,1)S(1)} %copy.282), channel_id=1, replica_groups=mesh['req'=4,'exp'=32] {'exp'}, dimensions={1} | all-to-all | bytes 10485760 | tf_op jit(solution)/shard_map/all_to_all | solution.py:153
  176.5 8.2 %fusion.19 = f32[2,32,1,40,1024]{4,3,1,0,2:T(8,128)} fusion(bf16[2,1,1024,1024]{3,2,1,0:T(8,128)(2,1)S(1)} %copy-done.20, bf16[2,32,40,1024]{3,2,0,1:T(8,128)(2,1)S(1)} %all_to_all.10), kind=kOutput, calls=%fused_computation.34 | convolution fusion | flops 5368709120 | bytes 19922944 | tf_op jit(solution)/shard_map/mslcd,mldf->mslcf/dot_general | solution.py:161
  184.7 7.2 %convolution_convert_fusion = bf16[2,32,40,1024]{3,2,1,0:T(8,128)(2,1)S(1)} fusion(f32[2,32,1,40,1024]{4,3,1,0,2:T(8,128)} %fusion.19, bf16[2,1,512,1024]{3,2,1,0:T(8,128)(2,1)S(1)} %copy-done), kind=kOutput, calls=%fused_computation.35 | convolution fusion | flops 2694840320 | bytes 17825792 | tf_op jit(solution)/shard_map/mslcf,mlfd->mslcd/dot_general | solution.py:163
  213.5 5.0 all-to-all-start.1
  218.7 61.7 %all-to-all-done.1 = bf16[32,2,1,40,1024]{4,3,1,2,0:T(8,128)(2,1)} async-done(((bf16[32,2,1,40,1024]{4,3,1,2,0:T(8,128)(2,1)}), bf16[32,2,1,40,1024]{4,3,1,2,0:T(8,128)(2,1)}, u32[]{:S(2)}, u32[]{:S(2)}) %all-to-all-start.1) | async-done | bytes 5242912 | tf_op jit(solution)/shard_map/all_to_all | solution.py:167
  280.4 5.6 copy.315
  286.0 14.1 %gather_fusion.1 = bf16[2048,1024]{1,0:T(8,128)(2,1)} fusion(bf16[2560,1024]{1,0:T(8,128)(2,1)} %bitcast.422, s32[2048]{0:T(1024)S(1)} %broadcast_clamp_fusion), kind=kCustom, calls=%fused_computation.1 | custom fusion | bytes 8396800 | tf_op jit(solution)/shard_map/gather | solution.py:181
  300.1 4.8 fusion.8
  306.3 73.6 %all-gather.5.cloned.1.call-done = bf16[2,4096,1024]{2,1,0:T(8,128)(2,1)} async-done(((bf16[2,128,1024]{2,1,0:T(8,128)(2,1)}), bf16[2,4096,1024]{2,1,0:T(8,128)(2,1)}) %all-gather.5.cloned.1.call-update) | async-done | bytes 16777232 | tf_op jit(solution)/shard_map/all_gather | solution.py:192
  379.9 79.6 %while.35 = (s32[]{:T(128)}, f32[8,2,512]{2,1,0:T(2,128)S(1)}, f32[8,2,512]{2,1,0:T(2,128)}, f32[8,2,512]{2,1,0:T(2,128)}, s32[8]{0:T(128)S(1)}, /*index=5*/bf16...) while((s32[]{:T(128)}, f32[8,2,512]{2,1,0:T(2,128)S(1)}, ...), condition=%wide.region_20.21_spmd.clone, body=%wide.region_16.20_spmd.clone.sunk | while | flops 2423583744 | bytes 17480380 | solution.py:212
  381.1 6.0 fusion.193
  387.6 1.6 select_reduce_fusion.5
  391.1 6.0 fusion.193
  397.6 1.6 select_reduce_fusion.5
  401.0 6.0 fusion.193
  407.5 1.6 select_reduce_fusion.5
  411.0 6.0 fusion.193
  417.4 1.6 select_reduce_fusion.5
  420.9 6.0 fusion.193
  427.4 1.6 select_reduce_fusion.5
  430.9 6.0 fusion.193
  437.4 1.6 select_reduce_fusion.5
  440.8 6.0 fusion.193
  447.3 1.6 select_reduce_fusion.5
  450.8 6.0 fusion.193
  457.3 1.6 select_reduce_fusion.5
  460.8 40.9 %all-gather.11.cloned.1.call-done = f32[32,2,4096]{2,1,0:T(2,128)} async-done(((f32[1,2,4096]{2,1,0:T(2,128)}), f32[32,2,4096]{2,1,0:T(2,128)}) %all-gather.11.cloned.1.call-update) | async-done | bytes 1048592 | tf_op jit(solution)/shard_map/all_gather | solution.py:21
  502.5 43.5 %all-gather.9.cloned.1.call-done = f32[32,2,4096]{2,1,0:T(2,128)} async-done(((f32[1,2,4096]{2,1,0:T(2,128)}), f32[32,2,4096]{2,1,0:T(2,128)}) %all-gather.9.cloned.1.call-update) | async-done | bytes 1048592 | tf_op jit(solution)/shard_map/all_gather | solution.py:21
  546.7 43.4 %all-gather.7.cloned.1.call-done = f32[32,2,4096]{2,1,0:T(2,128)} async-done(((f32[1,2,4096]{2,1,0:T(2,128)}), f32[32,2,4096]{2,1,0:T(2,128)}) %all-gather.7.cloned.1.call-update) | async-done | bytes 1048592 | tf_op jit(solution)/shard_map/all_gather | solution.py:21
  590.9 27.7 %while.34 = (s32[]{:T(128)}, f32[2,4096]{1,0:T(2,128)S(1)}, f32[2,4096]{1,0:T(2,128)S(1)}, f32[2,4096]{1,0:T(2,128)S(1)}, f32[32,2,4096]{2,1,0:T(2,128)}, /*inde...) while((s32[]{:T(128)}, f32[2,4096]{1,0:T(2,128)S(1)}, ...), condition=%wide.region_22.23_spmd, body=%wide.region_21.22_spmd.sunk | while | flops 57349 | bytes 295059 | solution.py:27
  618.8 64.1 %all-reduce = f32[512]{0:T(512)S(1)} all-reduce(f32[512]{0:T(512)S(1)} %select_reduce_fusion.1), channel_id=2, replica_groups=mesh['req'=4,'exp'=32] {'req','exp'}, use_global_device_ids=true, to_apply=%region_25.26.clone | all-reduce | flops 512 | bytes 4096
  (226 shorter events, 81.6 us)
Async XLA Ops:
  7.2 177.5 %copy-start = (bf16[2,1,512,1024]{3,2,1,0:T(8,128)(2,1)S(1)}, bf16[2,1,512,1024]{3,2,1,0:T(8,128)(2,1)}, u32[]{:S(2)}) copy-start(bf16[2,1,512,1024]{3,2,1,0:T(8,128)(2,1)} %param.26) | copy-start | bytes 6291460
  9.3 5.2 copy-start.21
  12.4 1.0 copy-start.2
  14.9 0.6 copy-start.15
  24.7 1.0 copy-start.3
  25.6 6.6 copy-start.11
  25.6 7.2 %copy-start.8 = (s32[2,128,8]{1,2,0:T(8,128)S(1)}, s32[2,128,8]{1,2,0:T(8,128)}, u32[]{:S(2)}) copy-start(s32[2,128,8]{1,2,0:T(8,128)} %param.19) | copy-start | bytes 24580
  31.2 8.2 %copy-start.4 = (bf16[2,128,1024]{2,1,0:T(8,128)(2,1)S(1)}, bf16[2,128,1024]{2,1,0:T(8,128)(2,1)}, u32[]{:S(2)}) copy-start(bf16[2,128,1024]{2,1,0:T(8,128)(2,1)} %param.16) | copy-start | bytes 1572868
  36.7 7.7 %copy-start.5 = (bf16[2,128,1024]{2,1,0:T(8,128)(2,1)S(1)}, bf16[2,128,1024]{2,1,0:T(8,128)(2,1)}, u32[]{:S(2)}) copy-start(bf16[2,128,1024]{2,1,0:T(8,128)(2,1)} %param.16) | copy-start | bytes 1572868
  41.6 5.9 copy-start.13
  63.3 5.6 copy-start.7
  63.3 24.2 %copy-start.6 = (s32[2,1024]{1,0:T(2,128)S(1)}, s32[2,1024]{1,0:T(2,128)}, u32[]{:S(2)}) copy-start(s32[2,1024]{1,0:T(2,128)} %eq.95) | copy-start | bytes 24580
  63.3 24.3 %copy-start.9 = (s32[2,128,8]{1,2,0:T(8,128)S(1)}, s32[2,128,8]{1,2,0:T(8,128)}, u32[]{:S(2)}) copy-start(s32[2,128,8]{1,2,0:T(8,128)} %broadcast_multiply_fusion.1) | copy-start | bytes 24580
  63.3 24.6 %copy-start.18 = (s32[2]{0:T(128)S(1)}, s32[2]{0:T(128)}, u32[]{:S(2)}) copy-start(s32[2]{0:T(128)} %iota_multiply_fusion) | copy-start | bytes 28
  105.0 71.5 %copy-start.20 = (bf16[2,1,1024,1024]{3,2,1,0:T(8,128)(2,1)S(1)}, bf16[2,1,1024,1024]{3,2,1,0:T(8,128)(2,1)}, u32[]{:S(2)}) copy-start(bf16[2,1,1024,1024]{3,2,1,0:T(8,128)(2,1)} %param.25) | copy-start | bytes 12582916
  213.5 5.0 copy-start.14
  213.5 66.9 %all-to-all-start.1 = ((bf16[32,2,1,40,1024]{4,3,1,2,0:T(8,128)(2,1)}), bf16[32,2,1,40,1024]{4,3,1,2,0:T(8,128)(2,1)}, u32[]{:S(2)}, u32[]{:S(2)}) async-start(bf16[32,2,1,40,1024]{4,3,1,2,0:T(8,128)(2,1)} %fusion.104), calls=%async_computation.1 | async-start | bytes 10485760 | tf_op jit(solution)/shard_map/all_to_all | solution.py:167
  218.5 161.4 %all-gather.5.cloned.1.call-start = ((), (), s32[]{:S(2)}) async-start(), calls=%async_computation.2 | async-start | bytes 17301504 | tf_op jit(solution)/shard_map/all_gather | solution.py:192
  300.1 6.2 copy-start.12
  306.2 195.5 %all-gather.11.cloned.1.call-start = ((), (), s32[]{:S(2)}) async-start(), calls=%async_computation.5 | async-start | bytes 1081344 | tf_op jit(solution)/shard_map/all_gather | solution.py:21
  379.9 238.7 %copy-start.16 = (s32[128]{0:T(128)S(1)}, s32[128]{0:T(128)}, u32[]{:S(2)}) copy-start(s32[128]{0:T(128)} %copy-done.15) | copy-start | bytes 1540
  379.9 238.8 %copy-start.19 = (s32[4]{0:T(128)S(1)}, s32[4]{0:T(128)}, u32[]{:S(2)}) copy-start(s32[4]{0:T(128)} %param.21) | copy-start | bytes 52
  459.5 0.8 copy-start.10
  459.5 224.0 %copy-start.1 = (bf16[2,1,512,1024]{3,2,1,0:T(8,128)(2,1)S(1)}, bf16[2,1,512,1024]{3,2,1,0:T(8,128)(2,1)}, u32[]{:S(2)}) copy-start(bf16[2,1,512,1024]{3,2,1,0:T(8,128)(2,1)} %param.26) | copy-start | bytes 6291460
  459.5 86.5 %all-gather.9.cloned.1.call-start = ((), (), s32[]{:S(2)}) async-start(), calls=%async_computation.4 | async-start | bytes 1081344 | tf_op jit(solution)/shard_map/all_gather | solution.py:21
  460.3 129.8 %all-gather.7.cloned.1.call-start = ((), (), s32[]{:S(2)}) async-start(), calls=%async_computation.3 | async-start | bytes 1081344 | tf_op jit(solution)/shard_map/all_gather | solution.py:21
  618.5 65.0 %copy-start.17 = (f32[2,128]{1,0:T(2,128)}, f32[2,128]{1,0:T(2,128)S(1)}, u32[]{:S(2)}) copy-start(f32[2,128]{1,0:T(2,128)S(1)} %add_subtract_fusion) | copy-start | bytes 3076
Sparse Core Ops, SparseCore 0:
  306.3 73.5 all-gather.4
  459.6 42.0 all-gather.10
  504.0 41.9 all-gather.8
  548.1 41.9 all-gather.6
